TPU v7x, 512 devices: a whole 4x8x8 slice. The times are simulated.
512 devices in a mesh: dp: 4 (over z_lo, core), ctx: 128 (over x, y, z_hi).
Axes of the slice: x: 4, y: 8, z: 8 (z_hi: 4, z_lo: 2; z = z_hi * 2 + z_lo), core: 2. Of those that a mesh axis runs over, the one named last changes fastest.
Arguments:
- query: bfloat16 [4, 32768, 1024], P('dp', 'ctx'), may hold values from -150 to 150
- key: bfloat16 [4, 32768, 1024], P('dp', 'ctx'), may hold values from -3 to 3
- value: bfloat16 [4, 32768, 1024], P('dp', 'ctx'), may hold values from -6 to 6
- grad_out: bfloat16 [4, 32768, 1024], P('dp', 'ctx'), may hold values from -30 to 30
- clause: int32 [4, 32768], P('dp', 'ctx'), may hold values from 0 to 2047, never falling along the last dimension, each value on 1 to 48 neighbouring positions
- bias_table: float32 [32, 2], replicated, may hold values from -1.5 to 1.5
Outputs:
- attended: bfloat16 [4, 32768, 1024], P('dp', 'ctx')
- query_gradient: bfloat16 [4, 32768, 1024], P('dp', 'ctx')
- key_gradient: bfloat16 [4, 32768, 1024], P('dp', 'ctx')
- value_gradient: bfloat16 [4, 32768, 1024], P('dp', 'ctx')
- bias_grad: float32 [32, 2], replicated
Inputs may be any that keep to these rules, and one draw needn't show every extreme that they name: Clause ids never fall along a document; a clause holds 1 to 48 tokens, and some clause holds exactly 48.
All inputs are finite; a program needn't handle non-finite values.
Results may differ from a plain program's by a relative error of at most 0.009.
Values may be sent and summed in bfloat16 or wider, within the bound.
No kernel may reach another device: no remote copies, remote signals or barrier semaphores. Data moves between devices by JAX's collectives and lax.ppermute only.
A program may use at most 128 MiB of HBM per device.

v0:
```python
import jax
import jax.numpy as jnp
from jax import lax
from jax.sharding import Mesh, PartitionSpec as P

HEADS = 8
WINDOW = 512
BUCKETS = 32
DILATION_FIRST = 1
DILATION_SECOND = 8
DILATION_THIRD = 32
CTX = ("cx", "cy", "cz")


def swapped(block, axis, bit):
    count = lax.axis_size(axis)
    route = []
    for low in range(count):
        high = low | 1 << bit
        if high != low and high < count:
            route += [(low, high), (high, low)]
    return lax.ppermute(block, axis, route)


def shifted(value, axis, steps):
    count = lax.axis_size(axis)
    leading, last = (max(0, -steps), min(count, count - steps))
    return lax.ppermute(value, axis, [(source, source + steps) for source in range(leading, last)])


def with_halo(shard, sides, width):
    for axis, dim in sides:
        size, length = (lax.axis_size(axis), shard.shape[dim])
        up = [(i, (i + 1) % size) for i in range(size - 1)]
        down = [(j, i) for i, j in up]
        last = lax.slice_in_dim(shard, length - width, length, axis=dim)
        leading = lax.slice_in_dim(shard, 0, width, axis=dim)
        before = lax.ppermute(last, axis, up)
        after = lax.ppermute(leading, axis, down)
        shard = jnp.concatenate([before, shard, after], axis=dim)
    return shard


def sample_rows(matrix, initial_flag, dilation_rate):
    count = matrix.shape[0] // dilation_rate
    head_dim = matrix.shape[1] // HEADS
    grid = matrix.reshape(count, dilation_rate, HEADS, head_dim)
    return jnp.concatenate(
        [grid[:, 0, initial_flag], grid[:, dilation_rate // 2, initial_flag + 1]], axis=1
    )


def spread_rows(sampled, dilation_rate):
    count = sampled.shape[0]
    grid = jnp.zeros((count, dilation_rate) + sampled.shape[1:], sampled.dtype)
    grid = grid.at[:, 0, 0].set(sampled[:, 0]).at[:, dilation_rate // 2, 1].set(sampled[:, 1])
    return grid.reshape((count * dilation_rate,) + sampled.shape[1:])


def upper_half(bit):
    index = lax.axis_index(CTX)
    return index // 2**bit % 2 == 1


def double_rows(block, bits):
    for bit in range(bits):
        other = swapped(block, CTX, bit)
        block = jnp.where(
            upper_half(bit),
            jnp.concatenate([other, block], axis=0),
            jnp.concatenate([block, other], axis=0),
        )
    return block


def halve_sums(block, bits):
    for bit in reversed(range(bits)):
        half = block.shape[0] // 2
        lower, higher = (block[:half], block[half:])
        upper = upper_half(bit)
        outgoing = jnp.where(upper, lower, higher)
        staying = jnp.where(upper, higher, lower)
        block = staying + swapped(outgoing.astype(jnp.bfloat16), CTX, bit).astype(outgoing.dtype)
    return block


def span_rows(block, bits):
    return double_rows(block, bits)


def span_sums(block, bits):
    return halve_sums(block, bits)


def rows_side(score_matrix, every_key_rows, every_value_rows, gradient_list, score_scale):
    top = jnp.max(score_matrix, axis=-1, keepdims=True)
    raised = jnp.exp(score_matrix - top)
    totals = jnp.sum(raised, axis=-1, keepdims=True)
    shares = raised / totals
    softmax_weights = shares.astype(jnp.bfloat16)
    attended = jnp.einsum(
        "ezb,beo->zeo", softmax_weights, every_value_rows, preferred_element_type=jnp.float32
    )
    weight_gradient = jnp.einsum(
        "wvx,yvx->vwy", gradient_list, every_value_rows, preferred_element_type=jnp.float32
    )
    delta = jnp.sum(shares * weight_gradient, axis=-1, keepdims=True)
    logit_grads = shares * (weight_gradient - delta)
    score_gradient = logit_grads.astype(jnp.bfloat16)
    query_gradient = (
        jnp.einsum(
            "ezb,beo->zeo", score_gradient, every_key_rows, preferred_element_type=jnp.float32
        )
        * score_scale
    )
    return (
        attended,
        query_gradient,
        softmax_weights,
        score_gradient,
        logit_grads,
        top,
        totals,
        delta,
    )


def keys_side(softmax_weights, score_gradient, query_matrix, gradient_list, score_scale):
    key_gradient = (
        jnp.einsum("vjb,jvw->bvw", score_gradient, query_matrix, preferred_element_type=jnp.float32)
        * score_scale
    )
    value_gradient = jnp.einsum(
        "vjb,jvw->bvw", softmax_weights, gradient_list, preferred_element_type=jnp.float32
    )
    return (key_gradient, value_gradient)


def bucket_lookup(bucket, table):
    running = jnp.zeros((table.shape[1],) + bucket.shape, jnp.float32)
    for level in range(BUCKETS):
        running = jnp.where(bucket[None] == level, table[level][:, None, None], running)
    return running


def bucket_sums(bucket, logit_grads):
    totals = [
        jnp.sum(jnp.where(bucket[None] == level, logit_grads, 0.0), axis=(1, 2))
        for level in range(BUCKETS)
    ]
    return jnp.stack(totals, axis=0)


def pass_rim(rim, offset):
    return shifted(rim.astype(jnp.bfloat16), CTX, offset).astype(rim.dtype)


def band_part(query_rows, key_rows, value_rows, grad_rows, clause_rows, table, score_scale):
    rows, width = query_rows.shape
    head_dim = width // HEADS
    wide = 2 * head_dim
    half = WINDOW // 2
    pair_rows = jnp.concatenate([key_rows[:, :wide], value_rows[:, :wide]], axis=1)
    extended, extended_clause = (
        with_halo(pair_rows, ((CTX, 0),), half),
        with_halo(clause_rows, ((CTX, 0),), half),
    )
    reach = rows + 2 * half
    nearby_key_rows = extended[:, :wide].reshape(reach, 2, head_dim)
    values_near = extended[:, wide:].reshape(reach, 2, head_dim)
    query_matrix = query_rows[:, :wide].reshape(rows, 2, head_dim)
    gradient_list = grad_rows[:, :wide].reshape(rows, 2, head_dim)
    start = lax.axis_index(CTX) * rows
    length = rows * lax.axis_size(CTX)
    local_query = jnp.arange(rows)[:, None]
    local_key = jnp.arange(reach)[None, :] - half
    global_key = start + local_key
    allowed = (jnp.abs(local_query - local_key) < half) & (global_key >= 0) & (global_key < length)
    bucket = jnp.minimum(jnp.abs(clause_rows[:, None] - extended_clause[None, :]), BUCKETS - 1)
    score_matrix = (
        jnp.einsum(
            "wvx,yvx->vwy", query_matrix, nearby_key_rows, preferred_element_type=jnp.float32
        )
        * score_scale
    )
    score_matrix = jnp.where(allowed[None], score_matrix + bucket_lookup(bucket, table), -jnp.inf)
    attended, query_gradient, softmax_weights, score_gradient, logit_grads, top, totals, delta = (
        rows_side(score_matrix, nearby_key_rows, values_near, gradient_list, score_scale)
    )
    key_gradient, value_gradient = keys_side(
        softmax_weights, score_gradient, query_matrix, gradient_list, score_scale
    )
    sums = jnp.concatenate(
        [key_gradient.reshape(reach, wide), value_gradient.reshape(reach, wide)], axis=1
    )
    own = sums[half : half + rows]
    from_next = pass_rim(sums[:half], -1)
    from_prev = pass_rim(sums[half + rows :], 1)
    own = own.at[rows - half :].add(from_next).at[:half].add(from_prev)
    own_key = own[:, :wide].reshape(rows, 2, head_dim)
    own_value = own[:, wide:].reshape(rows, 2, head_dim)
    return (attended, query_gradient, own_key, own_value, bucket_sums(bucket, logit_grads))


def dilated(
    query_rows, key_rows, value_rows, grad_rows, initial_flag, dilation_rate, bits, score_scale
):
    head_dim = query_rows.shape[1] // HEADS
    wide = 2 * head_dim
    picked_query = sample_rows(query_rows, initial_flag, dilation_rate)
    picked_key = sample_rows(key_rows, initial_flag, dilation_rate)
    picked_value = sample_rows(value_rows, initial_flag, dilation_rate)
    picked_grad = sample_rows(grad_rows, initial_flag, dilation_rate)
    count = picked_query.shape[0]
    gathered = lax.all_gather(
        jnp.concatenate([picked_key, picked_value], axis=1), bits, axis=0, tiled=True
    )
    gathered_rows = gathered.shape[0]
    every_key_rows = gathered[:, :wide].reshape(gathered_rows, 2, head_dim)
    every_value_rows = gathered[:, wide:].reshape(gathered_rows, 2, head_dim)
    query_matrix = picked_query.reshape(count, 2, head_dim)
    gradient_list = picked_grad.reshape(count, 2, head_dim)
    score_matrix = (
        jnp.einsum("wvx,yvx->vwy", query_matrix, every_key_rows, preferred_element_type=jnp.float32)
        * score_scale
    )
    attended, query_gradient, softmax_weights, score_gradient, logit_grads, top, totals, delta = (
        rows_side(score_matrix, every_key_rows, every_value_rows, gradient_list, score_scale)
    )
    key_gradient, value_gradient = keys_side(
        softmax_weights, score_gradient, query_matrix, gradient_list, score_scale
    )
    partial_sums = jnp.concatenate(
        [key_gradient.reshape(gathered_rows, wide), value_gradient.reshape(gathered_rows, wide)],
        axis=1,
    )
    own = lax.psum_scatter(partial_sums, bits, scatter_dimension=0, tiled=True)
    own_key = own[:, :wide].reshape(count, 2, head_dim)
    own_value = own[:, wide:].reshape(count, 2, head_dim)
    return (
        spread_rows(attended, dilation_rate),
        spread_rows(query_gradient, dilation_rate),
        spread_rows(own_key, dilation_rate),
        spread_rows(own_value, dilation_rate),
    )


def shards(query, key, value, grad_out, clause, bias_table):
    query_rows = query[0]
    key_rows = key[0]
    value_rows = value[0]
    grad_rows = grad_out[0]
    clause_rows = clause[0]
    rows, width = query_rows.shape
    head_dim = width // HEADS
    score_scale = head_dim ** (-0.5)
    band = band_part(
        query_rows, key_rows, value_rows, grad_rows, clause_rows, bias_table, score_scale
    )
    pieces = [band[:4]]
    for initial_flag, dilation_rate, bits in (
        (2, DILATION_FIRST, CTX[2:]),
        (4, DILATION_SECOND, CTX[1:]),
        (6, DILATION_THIRD, CTX),
    ):
        pieces.append(
            dilated(
                query_rows,
                key_rows,
                value_rows,
                grad_rows,
                initial_flag,
                dilation_rate,
                bits,
                score_scale,
            )
        )
    bias_grad = lax.psum(band[4], ("dp",) + CTX)
    joined = [
        jnp.concatenate([piece[slot] for piece in pieces], axis=1)
        .reshape(1, rows, width)
        .astype(jnp.bfloat16)
        for slot in range(4)
    ]
    return (joined[0], joined[1], joined[2], joined[3], bias_grad)


def solution(mesh):
    ctx_size = mesh.shape["ctx"]
    parts = (4, 8, ctx_size // 32)
    split = Mesh(mesh.devices.reshape((mesh.shape["dp"],) + parts), ("dp",) + CTX)
    in_specs = (
        P("dp", CTX, None),
        P("dp", CTX, None),
        P("dp", CTX, None),
        P("dp", CTX, None),
        P("dp", CTX),
        P(),
    )
    out_specs = (
        P("dp", CTX, None),
        P("dp", CTX, None),
        P("dp", CTX, None),
        P("dp", CTX, None),
        P(),
    )
    return jax.shard_map(
        shards, mesh=split, in_specs=in_specs, out_specs=out_specs, check_vma=False
    )
```

profile of v0, /device:TPU:64, one launch (start us, length us, event | category | flops | bytes accessed | tf_op | source)
XLA Modules:
  0.0 1330.2 jit_solution(18316485275672854321)
XLA Ops:
  7.2 1.3 copy.505
  8.5 1.3 copy.506
  11.7 1.3 collective-permute-start.3
  13.0 6.7 collective-permute-start.2
  20.5 1.3 collective-permute-start.1
  21.8 7.8 collective-permute-start
  34.0 1.4 fusion.55
  40.6 5.3 fusion.53
  46.3 5.0 collective-permute-done
  53.0 5.7 fusion.9
  60.4 5.5 select_reduce_fusion
  65.9 4.6 all-gather.4.cloned.1.call-done
  71.8 3.7 fusion.132
  75.5 3.2 fusion.60
  78.7 2.3 multiply_reduce_fusion
  83.2 1.5 pad_maximum_fusion
  84.7 5.4 select_reduce_fusion.18
  90.1 1.3 copy.601
  91.5 1.3 copy.602
  92.8 1.3 copy.583
  94.1 1.3 copy.584
  99.1 1.3 copy.597
  100.4 1.3 copy.596
  101.7 1.3 copy.595
  104.3 1.3 copy.593
  108.0 1.3 copy.590
  109.3 1.4 copy.589
  110.6 1.3 copy.588
  116.9 1.3 copy.581
  121.9 1.3 copy.577
  123.2 1.3 copy.576
  125.8 1.3 copy.574
  127.1 1.3 copy.573
  130.9 3.4 fusion.65
  136.6 1.3 collective-permute-start.4
  137.9 6.2 collective-permute-start.5
  145.2 103.3 %psum.7 = f32[32,2]{0,1:T(2,128)} all-reduce(f32[32,2]{0,1:T(2,128)S(1)} %stack.131), channel_id=1, replica_groups=mesh['dp'=4,'cx'=4,'cy'=8,'cz'=4] {'dp','cx','cy','cz'}, use_global_device_ids=true, to_apply=%region_47.48 | all-reduce | flops 64 | bytes 512 | tf_op jit(solution)/shard_map/psum | solution.py:278
  248.4 3.2 fusion.15
  251.6 2.0 fusion.16
  255.7 2.0 convolution_bitcast_fusion
  260.4 1.4 fusion.71
  263.1 1.8 copy.629
  268.9 6.5 all-gather.8.cloned.1.call-done
  278.3 1.3 fusion.77
  281.0 1.9 copy.631
  286.6 38.0 %reduce-scatter.8.cloned.1.call-done = f32[256,512]{0,1:T(8,128)} async-done(((f32[1024,512]{0,1:T(8,128)}), f32[256,512]{0,1:T(8,128)}) %reduce-scatter.8.cloned.1.call-update) | async-done | bytes 524304 | tf_op jit(solution)/shard_map/reduce_scatter | solution.py:237
  327.1 233.6 %reduce-scatter.10.cloned.1.call-done = f32[32,512]{1,0:T(8,128)} async-done(((f32[1024,512]{1,0:T(8,128)}), f32[32,512]{1,0:T(8,128)}) %reduce-scatter.10.cloned.1.call-update) | async-done | bytes 65552
  562.5 757.5 %reduce-scatter.12.cloned.1.call-done = f32[8,512]{1,0:T(8,128)} async-done(((f32[1024,512]{1,0:T(8,128)}), f32[8,512]{1,0:T(8,128)}) %reduce-scatter.12.cloned.1.call-update) | async-done | bytes 16400 | tf_op jit(solution)/shard_map/reduce_scatter | solution.py:237
  (433 shorter events, 66.3 us)
Async XLA Ops:
  7.2 63.3 %all-gather.4.cloned.1.call-start = ((), (), s32[]{:S(2)}) async-start(), calls=%async_computation.3 | async-start | bytes 1310720 | tf_op jit(solution)/shard_map/all_gather | solution.py:215
  10.6 247.0 %all-gather.6.cloned.1.call-start = ((), (), s32[]{:S(2)}) async-start(), calls=%async_computation.4 | async-start | bytes 1081344 | tf_op jit(solution)/shard_map/all_gather | solution.py:215
  10.7 19.7 %copy-start.16 = (f32[32,2]{0,1:T(2,128)S(1)}, f32[32,2]{0,1:T(2,128)}, u32[]{:S(2)}) copy-start(f32[32,2]{0,1:T(2,128)} %param.67) | copy-start | bytes 772
  10.8 20.6 %copy-start.9 = (bf16[1,256,1024]{2,1,0:T(8,128)(2,1)S(1)}, bf16[1,256,1024]{2,1,0:T(8,128)(2,1)}, u32[]{:S(2)}) copy-start(bf16[1,256,1024]{2,1,0:T(8,128)(2,1)} %param.65) | copy-start | bytes 1572868
  11.7 263.7 %all-gather.8.cloned.1.call-start = ((), (), s32[]{:S(2)}) async-start(), calls=%async_computation.5 | async-start | bytes 1056768 | tf_op jit(solution)/shard_map/all_gather | solution.py:215
  11.7 28.8 %collective-permute-start.3 = (s32[256]{0:T(256)S(1)}, s32[256]{0:T(256)S(1)}, u32[]{:S(2)}, u32[]{:S(2)}) collective-permute-start(s32[256]{0:T(256)S(1)} %bitcast.406), channel_id=1, source_target_pairs={{1,0},{2,1},{3,2},{4,3},{5,4},{6,5},{7,6},{8,7},{9,8},{10,9},{11,1... | collective-permute-start | bytes 3080 | tf_op jit(solution)/shard_map/ppermute | solution.py:39
  13.0 27.6 %collective-permute-start.2 = (s32[256]{0:T(256)S(1)}, s32[256]{0:T(256)S(1)}, u32[]{:S(2)}, u32[]{:S(2)}) collective-permute-start(s32[256]{0:T(256)S(1)} %bitcast.407), channel_id=1, source_target_pairs={{0,1},{1,2},{2,3},{3,4},{4,5},{5,6},{6,7},{7,8},{8,9},{9,10},{10,1... | collective-permute-start | bytes 3080 | tf_op jit(solution)/shard_map/ppermute | solution.py:38
  19.8 12.0 copy-start.10
  20.5 25.8 %collective-permute-start.1 = (bf16[256,512]{0,1:T(8,128)(2,1)}, bf16[256,512]{0,1:T(8,128)(2,1)}, u32[]{:S(2)}, u32[]{:S(2)}) collective-permute-start(bf16[256,512]{0,1:T(8,128)(2,1)} %pad_maximum_fusion.9), channel_id=1, source_target_pairs={{1,0},{2,1},{3,2},{4,3},{5,4},{6,5},{7,6},{8,7},{9,8},{10,9},{11,1... | collective-permute-start | bytes 786440 | tf_op jit(solution)/shard_map/ppermute | solution.py:39
  21.8 29.5 %collective-permute-start = (bf16[256,512]{0,1:T(8,128)(2,1)}, bf16[256,512]{0,1:T(8,128)(2,1)}, u32[]{:S(2)}, u32[]{:S(2)}) collective-permute-start(bf16[256,512]{0,1:T(8,128)(2,1)} %pad_maximum_fusion.9), channel_id=1, source_target_pairs={{0,1},{1,2},{2,3},{3,4},{4,5},{5,6},{6,7},{7,8},{8,9},{9,10},{10,1... | collective-permute-start | bytes 786440 | tf_op jit(solution)/shard_map/ppermute | solution.py:38
  30.3 294.3 %reduce-scatter.8.cloned.1.call-start = ((), (), s32[]{:S(2)}) async-start(), calls=%async_computation.6 | async-start | bytes 2621440 | tf_op jit(solution)/shard_map/reduce_scatter | solution.py:237
  84.7 476.0 %reduce-scatter.10.cloned.1.call-start = ((), (), s32[]{:S(2)}) async-start(), calls=%async_computation.7 | async-start | bytes 2162688
  135.4 8.7 copy-start.62
  135.4 8.7 copy-start.63
  135.4 8.7 copy-start.64
  135.4 8.7 copy-start.65
  135.4 8.7 copy-start.66
  135.5 8.7 copy-start.67
  135.5 8.7 copy-start.68
  135.5 8.7 copy-start.69
  135.5 8.7 copy-start.70
  135.5 8.7 copy-start.71
  135.5 8.7 copy-start.72
  135.5 8.7 copy-start.73
  135.5 8.7 copy-start.74
  135.5 8.7 copy-start.75
  135.5 8.7 copy-start.76
  135.6 8.7 copy-start.77
  135.6 8.7 copy-start.78
  135.6 8.7 copy-start.79
  135.6 8.7 copy-start.80
  135.6 8.7 copy-start.81
  135.6 8.7 copy-start.82
  135.6 8.7 copy-start.83
  135.6 8.7 copy-start.84
  135.6 8.7 copy-start.85
  135.6 8.7 copy-start.86
  135.7 8.7 copy-start.87
  135.7 8.7 copy-start.88
  135.7 8.7 copy-start.89
  135.7 8.7 copy-start.90
  135.7 8.7 copy-start.91
  135.7 112.7 %copy-start.58 = (f32[2,256]{1,0:T(2,128)S(1)}, f32[2,256]{1,0:T(2,128)}, u32[]{:S(2)}) copy-start(f32[2,256]{1,0:T(2,128)} %copy-done.57) | copy-start | bytes 6148
  136.6 117.0 %collective-permute-start.4 = (bf16[256,512]{0,1:T(8,128)(2,1)}, bf16[256,512]{0,1:T(8,128)(2,1)}, u32[]{:S(2)}, u32[]{:S(2)}) collective-permute-start(bf16[256,512]{0,1:T(8,128)(2,1)} %get-tuple-element.444), channel_id=1, source_target_pairs={{1,0},{2,1},{3,2},{4,3},{5,4},{6,5},{7,6},{8,7},{9,8},{10,9},{11,1... | collective-permute-start | bytes 786440 | tf_op jit(solution)/shard_map/ppermute | solution.py:28
  137.9 115.7 %collective-permute-start.5 = (bf16[256,512]{0,1:T(8,128)(2,1)}, bf16[256,512]{0,1:T(8,128)(2,1)}, u32[]{:S(2)}, u32[]{:S(2)}) collective-permute-start(bf16[256,512]{0,1:T(8,128)(2,1)} %get-tuple-element.445), channel_id=1, source_target_pairs={{0,1},{1,2},{2,3},{3,4},{4,5},{5,6},{6,7},{7,8},{8,9},{9,10},{10,1... | collective-permute-start | bytes 786440 | tf_op jit(solution)/shard_map/ppermute | solution.py:28
  265.0 1055.0 %reduce-scatter.12.cloned.1.call-start = ((), (), s32[]{:S(2)}) async-start(), calls=%async_computation.8 | async-start | bytes 2113536 | tf_op jit(solution)/shard_map/reduce_scatter | solution.py:237
  267.5 9.2 copy-start.33
  561.8 759.4 %copy-start.38 = (bf16[256,256]{0,1:T(8,128)(2,1)S(1)}, bf16[256,256]{0,1:T(8,128)(2,1)}, u32[]{:S(2)}) copy-start(bf16[256,256]{0,1:T(8,128)(2,1)} %get-tuple-element.482) | copy-start | bytes 393220
  (88 other events, 384.2 us)
Sparse Core Ops, SparseCore 0:
  10.7 59.6 all-gather.3
  73.6 80.2 all-gather.5
  158.3 117.0 all-gather.7
  278.1 46.4 reduce-scatter.7
  329.6 231.0 reduce-scatter.9
  563.3 756.6 reduce-scatter.11
where the time goes:
time: 1330 us
  waiting for transfers between devices  1050 us (79%)
  blocking collectives  103 us (8%)
  local copies, waits for them, and re-layouts  80.6 us (6%)
  matrix products  32.6 us (2%)
  other arithmetic  26.9 us (2%)
  starting transfers between devices  24.9 us (2%)
  between operations  16.5 us (1%)
    reduce_scatter x2, waiting for transfers between devices, dilated(): own = lax.psum_scatter(partial_sums, bits, scatter_dimension=0, tiled=True)  796 us
    unnamed x7, waiting for transfers between devices  234 us
    psum x1, blocking collectives, shards(): bias_grad = lax.psum(band[4], ('dp',) + CTX)  103 us
    another operation x33, local copies, waits for them, and re-layouts, bucket_sums(): return jnp.stack(totals, axis=0)  41.6 us
  transfers between devices with their start and end apart: 12, of which 6 were waited for; matrix products, arithmetic and copies ran while one was open for 10% of the time, Pallas kernels for 0%

commit v1 on v0

--- a/solution.py
+++ b/solution.py
@@ -275,7 +275,7 @@
                 score_scale,
             )
         )
-    bias_grad = lax.psum(band[4], ("dp",) + CTX)
+    bias_grad = jnp.sum(lax.all_gather(band[4], ("dp",) + CTX), axis=0)
     joined = [
         jnp.concatenate([piece[slot] for piece in pieces], axis=1)
         .reshape(1, rows, width)

time: 1330 us -> 2700 us (2.03)
  blocking collectives: 103 us -> 1550 us
  waiting for transfers between devices: 1050 us -> 965 us
    all_gather x0 -> x1, blocking collectives: none -> 1550 us  [shards(): bias_grad = jnp.sum(lax.all_gather(band[4], ('dp',) + CTX), axis=0)]
    psum x1 -> x0, blocking collectives: 103 us -> none  [shards(): bias_grad = lax.psum(band[4], ('dp',) + CTX)]
    reduce_scatter x2, waiting for transfers between devices: 796 us -> 757 us  [dilated(): own = lax.psum_scatter(partial_sums, bits, scatter_dimension=0, tiled=True)]
    unnamed x7, waiting for transfers between devices: 234 us -> 201 us
  transfers between devices with their start and end apart: 12 -> 12, of which waited for: 6 -> 4; matrix products, arithmetic and copies ran while one was open for 10% -> 5% of each run, Pallas kernels for 0% -> 0%
where the time goes in v1:
time: 2700 us
  blocking collectives  1550 us (57%)
  waiting for transfers between devices  965 us (36%)
  local copies, waits for them, and re-layouts  83.1 us (3%)
  matrix products  32.3 us (1%)
  other arithmetic  30.7 us (1%)
    all_gather x1, blocking collectives, shards(): bias_grad = jnp.sum(lax.all_gather(band[4], ('dp',) + CTX), axis=0)  1550 us
    reduce_scatter x2, waiting for transfers between devices, dilated(): own = lax.psum_scatter(partial_sums, bits, scatter_dimension=0, tiled=True)  757 us
    unnamed x7, waiting for transfers between devices  201 us
  transfers between devices with their start and end apart: 12, of which 4 were waited for; matrix products, arithmetic and copies ran while one was open for 5% of the time, Pallas kernels for 0%

profile of v1, /device:TPU:64, one launch (start us, length us, event | category | flops | bytes accessed | tf_op | source)
XLA Modules:
  0.0 2702.0 jit_solution(6241908919485350767)
XLA Ops:
  7.2 1.3 copy.505
  8.5 1.3 copy.506
  12.5 1.3 collective-permute-start.3
  13.8 6.7 collective-permute-start.2
  21.3 1.3 collective-permute-start.1
  22.6 7.8 collective-permute-start
  35.6 1.4 fusion.55
  42.1 5.3 fusion.53
  47.9 4.2 collective-permute-done
  53.8 5.7 fusion.9
  61.1 5.6 select_reduce_fusion
  66.7 3.3 all-gather.6.cloned.1.call-done
  71.3 3.7 fusion.132
  75.1 3.2 fusion.60
  78.3 2.3 multiply_reduce_fusion
  82.7 1.5 pad_maximum_fusion
  84.3 5.4 select_reduce_fusion.18
  89.7 1.3 copy.601
  92.3 1.3 copy.583
  93.5 1.3 copy.584
  94.9 1.3 copy.600
  99.9 1.3 copy.596
  101.3 1.3 copy.595
  103.8 1.3 copy.593
  106.4 1.3 copy.591
  109.0 1.3 copy.589
  114.1 1.3 copy.585
  117.9 1.3 copy.580
  119.3 1.3 copy.579
  120.6 1.3 copy.578
  124.3 1.3 copy.575
  125.6 1.3 copy.574
  128.1 1.3 copy.572
  130.7 3.4 fusion.65
  136.4 1.3 collective-permute-start.4
  137.7 6.2 collective-permute-start.5
  145.0 1549.5 %all-gather.1 = f32[512,32,2]{1,2,0:T(2,128)} all-gather(f32[1,32,2]{1,2,0:T(2,128)S(1)} %bitcast.410), channel_id=2, replica_groups=mesh['dp'=4,'cx'=4,'cy'=8,'cz'=4] {'dp','cx','cy','cz'}, dimensions={0}, use_global_device_ids=true | all-gather | bytes 131328 | tf_op jit(solution)/shard_map/all_gather | solution.py:278
  1694.5 2.2 reduce_sum.409
  1696.6 3.2 fusion.15
  1699.8 2.0 fusion.16
  1703.8 2.0 convolution_bitcast_fusion
  1710.5 1.5 pad_maximum_fusion.1
  1712.0 2.9 copy.629
  1718.9 1.3 fusion.112
  1721.8 1.3 fusion.77
  1724.5 1.9 copy.631
  1732.6 200.8 %reduce-scatter.10.cloned.1.call-done = f32[32,512]{1,0:T(8,128)} async-done(((f32[1024,512]{1,0:T(8,128)}), f32[32,512]{1,0:T(8,128)}) %reduce-scatter.10.cloned.1.call-update) | async-done | bytes 65552
  1935.2 756.6 %reduce-scatter.12.cloned.1.call-done = f32[8,512]{1,0:T(8,128)} async-done(((f32[1024,512]{1,0:T(8,128)}), f32[8,512]{1,0:T(8,128)}) %reduce-scatter.12.cloned.1.call-update) | async-done | bytes 16400 | tf_op jit(solution)/shard_map/reduce_scatter | solution.py:237
  (426 shorter events, 67.3 us)
Async XLA Ops:
  7.2 62.9 %all-gather.6.cloned.1.call-start = ((), (), s32[]{:S(2)}) async-start(), calls=%async_computation.3 | async-start | bytes 1310720 | tf_op jit(solution)/shard_map/all_gather | solution.py:215
  10.6 1695.2 %all-gather.8.cloned.1.call-start = ((), (), s32[]{:S(2)}) async-start(), calls=%async_computation.4 | async-start | bytes 1081344 | tf_op jit(solution)/shard_map/all_gather | solution.py:215
  10.7 21.2 copy-start.13
  10.8 22.2 copy-start.6
  12.5 1706.4 %all-gather.10.cloned.1.call-start = ((), (), s32[]{:S(2)}) async-start(), calls=%async_computation.5 | async-start | bytes 1056768 | tf_op jit(solution)/shard_map/all_gather | solution.py:215
  12.5 29.6 %collective-permute-start.3 = (s32[256]{0:T(256)S(1)}, s32[256]{0:T(256)S(1)}, u32[]{:S(2)}, u32[]{:S(2)}) collective-permute-start(s32[256]{0:T(256)S(1)} %bitcast.407), channel_id=1, source_target_pairs={{1,0},{2,1},{3,2},{4,3},{5,4},{6,5},{7,6},{8,7},{9,8},{10,9},{11,1... | collective-permute-start | bytes 3080 | tf_op jit(solution)/shard_map/ppermute | solution.py:39
  13.8 28.3 %collective-permute-start.2 = (s32[256]{0:T(256)S(1)}, s32[256]{0:T(256)S(1)}, u32[]{:S(2)}, u32[]{:S(2)}) collective-permute-start(s32[256]{0:T(256)S(1)} %bitcast.408), channel_id=1, source_target_pairs={{0,1},{1,2},{2,3},{3,4},{4,5},{5,6},{6,7},{7,8},{8,9},{9,10},{10,1... | collective-permute-start | bytes 3080 | tf_op jit(solution)/shard_map/ppermute | solution.py:38
  20.6 12.8 copy-start.7
  21.3 26.6 collective-permute-start.1
  22.6 29.6 %collective-permute-start = (bf16[256,512]{0,1:T(8,128)(2,1)}, bf16[256,512]{0,1:T(8,128)(2,1)}, u32[]{:S(2)}, u32[]{:S(2)}) collective-permute-start(bf16[256,512]{0,1:T(8,128)(2,1)} %pad_maximum_fusion.9), channel_id=1, source_target_pairs={{0,1},{1,2},{2,3},{3,4},{4,5},{5,6},{6,7},{7,8},{8,9},{9,10},{10,1... | collective-permute-start | bytes 786440 | tf_op jit(solution)/shard_map/ppermute | solution.py:38
  31.8 1698.3 %reduce-scatter.8.cloned.1.call-start = ((), (), s32[]{:S(2)}) async-start(), calls=%async_computation.6 | async-start | bytes 2621440 | tf_op jit(solution)/shard_map/reduce_scatter | solution.py:237
  53.3 7.3 copy-start.35
  84.3 1849.1 %reduce-scatter.10.cloned.1.call-start = ((), (), s32[]{:S(2)}) async-start(), calls=%async_computation.7 | async-start | bytes 2162688
  135.2 8.7 copy-start.58
  135.2 8.7 copy-start.59
  135.2 8.7 copy-start.60
  135.2 8.7 copy-start.61
  135.2 8.7 copy-start.62
  135.2 8.7 copy-start.63
  135.2 8.7 copy-start.64
  135.2 8.7 copy-start.65
  135.2 8.7 copy-start.66
  135.3 8.7 copy-start.67
  135.3 8.7 copy-start.68
  135.3 8.7 copy-start.69
  135.3 8.7 copy-start.70
  135.3 8.7 copy-start.71
  135.3 8.7 copy-start.72
  135.3 8.7 copy-start.73
  135.3 8.7 copy-start.74
  135.3 8.7 copy-start.75
  135.3 8.7 copy-start.76
  135.4 8.7 copy-start.77
  135.4 8.7 copy-start.78
  135.4 8.7 copy-start.79
  135.4 8.7 copy-start.80
  135.4 8.7 copy-start.81
  135.4 8.7 copy-start.82
  135.4 8.7 copy-start.83
  135.4 8.7 copy-start.84
  135.4 8.7 copy-start.85
  135.4 8.7 copy-start.86
  135.5 8.7 copy-start.87
  135.6 1561.1 %copy-start.54 = (f32[2,256]{1,0:T(2,128)S(1)}, f32[2,256]{1,0:T(2,128)}, u32[]{:S(2)}) copy-start(f32[2,256]{1,0:T(2,128)} %copy-done.53) | copy-start | bytes 6148
  136.4 1565.4 %collective-permute-start.4 = (bf16[256,512]{0,1:T(8,128)(2,1)}, bf16[256,512]{0,1:T(8,128)(2,1)}, u32[]{:S(2)}, u32[]{:S(2)}) collective-permute-start(bf16[256,512]{0,1:T(8,128)(2,1)} %get-tuple-element.444), channel_id=1, source_target_pairs={{1,0},{2,1},{3,2},{4,3},{5,4},{6,5},{7,6},{8,7},{9,8},{10,9},{11,1... | collective-permute-start | bytes 786440 | tf_op jit(solution)/shard_map/ppermute | solution.py:28
  137.7 1564.2 %collective-permute-start.5 = (bf16[256,512]{0,1:T(8,128)(2,1)}, bf16[256,512]{0,1:T(8,128)(2,1)}, u32[]{:S(2)}, u32[]{:S(2)}) collective-permute-start(bf16[256,512]{0,1:T(8,128)(2,1)} %get-tuple-element.445), channel_id=1, source_target_pairs={{0,1},{1,2},{2,3},{3,4},{4,5},{5,6},{6,7},{7,8},{8,9},{9,10},{10,1... | collective-permute-start | bytes 786440 | tf_op jit(solution)/shard_map/ppermute | solution.py:28
  1715.0 976.8 %reduce-scatter.12.cloned.1.call-start = ((), (), s32[]{:S(2)}) async-start(), calls=%async_computation.8 | async-start | bytes 2113536 | tf_op jit(solution)/shard_map/reduce_scatter | solution.py:237
  1934.5 758.5 %copy-start.34 = (bf16[256,256]{0,1:T(8,128)(2,1)S(1)}, bf16[256,256]{0,1:T(8,128)(2,1)}, u32[]{:S(2)}) copy-start(bf16[256,256]{0,1:T(8,128)(2,1)} %get-tuple-element.482) | copy-start | bytes 393220
  (84 other events, 331.0 us)
Sparse Core Ops, SparseCore 0:
  10.7 59.2 all-gather.5
  73.2 79.1 all-gather.7
  156.8 111.4 all-gather.9
  271.0 46.6 reduce-scatter.7
  1715.1 218.2 reduce-scatter.9
  1936.0 755.7 reduce-scatter.11
